TPU v7x, 128 devices: a whole 4x4x4 slice. The times are simulated.
128 devices in a mesh: chan: 4 (over z_lo, core), blk: 32 (over z_hi, y, x).
Axes of the slice: x: 4, y: 4, z: 4 (z_hi: 2, z_lo: 2; z = z_hi * 2 + z_lo), core: 2. Of those that a mesh axis runs over, the one named last changes fastest.
Arguments:
- voltages: bfloat16 [256, 262144], P('blk', 'chan'), may hold values from -6 to 6
- fir_taps: float32 [8, 4096], replicated, may hold values from -2.1 to 2.1
Outputs:
- visibilities: float32 [2, 256, 256, 2048], P(None, 'blk', None, 'chan')
All inputs are finite; a program needn't handle non-finite values.
Results may differ from a plain program's by a relative error of at most 0.0036.
Values may be sent and summed in bfloat16 or wider, within the bound.
No kernel may reach another device: no remote copies, remote signals or barrier semaphores. Data moves between devices by JAX's collectives and lax.ppermute only.
A program may use at most 192 MiB of HBM per device.

v0:
```python
import math
import jax
import jax.numpy as jnp
from jax import lax
from jax.sharding import PartitionSpec as P

TAPS = 8
L = 4096
C = 2048


def shifted(value, axis, steps):
    count = lax.axis_size(axis)
    leading, last = (max(0, -steps), min(count, count - steps))
    return lax.ppermute(value, axis, [(source, source + steps) for source in range(leading, last)])


def dft_table(first_channel, channel_count, length):
    channel_ids = first_channel + jnp.arange(channel_count, dtype=jnp.int32)
    sample_ids = jnp.arange(length, dtype=jnp.int32)
    phase_index = sample_ids[:, None] * channel_ids[None, :] % length
    angles = phase_index.astype(jnp.float32) * (2.0 * math.pi / length)
    normaliser = 1.0 / math.sqrt(length)
    return jnp.concatenate([jnp.cos(angles) * normaliser, -jnp.sin(angles) * normaliser], axis=1)


def correlate_pair(left_block, right_block, inverse_count):
    gram_terms = jnp.einsum(
        "itpc,jtqc->ipjqc", left_block, right_block, preferred_element_type=jnp.float32
    )
    real_part = gram_terms[:, 0, :, 0] + gram_terms[:, 1, :, 1]
    imag_part = gram_terms[:, 1, :, 0] - gram_terms[:, 0, :, 1]
    return jnp.stack([real_part, imag_part]) * inverse_count


def on_device(voltages, fir_taps):
    feed_count = voltages.shape[0]
    frame_count = voltages.shape[1] // L
    own_frames = voltages.reshape(feed_count, frame_count, L)
    last_frames = own_frames[:, frame_count - (TAPS - 1) :, :]
    earlier = shifted(last_frames, "chan", 1)
    extended = jnp.concatenate([earlier, own_frames], axis=1)
    filtered = jnp.zeros((feed_count, frame_count, L), jnp.float32)
    for tap_index in range(TAPS):
        filtered = filtered + fir_taps[tap_index][None, None, :] * extended[
            :, tap_index : tap_index + frame_count, :
        ].astype(jnp.float32)
    frame_rows = filtered.reshape(feed_count * frame_count, L)
    block_width = min(C, 512)
    pieces = []
    for first_channel in range(0, C, block_width):
        cos_sin_table = dft_table(first_channel, block_width, L)
        product = jnp.dot(
            frame_rows,
            cos_sin_table,
            precision=lax.Precision.HIGHEST,
            preferred_element_type=jnp.float32,
        )
        pieces.append(product.reshape(feed_count * frame_count, 2, block_width))
    spectra = (
        jnp.concatenate(pieces, axis=2).astype(jnp.bfloat16).reshape(feed_count, frame_count, 2, C)
    )
    own_block = lax.all_to_all(spectra, "chan", split_axis=3, concat_axis=1, tiled=True)
    inverse_count = 1.0 / own_block.shape[1]
    return correlate_pair(
        own_block, lax.all_gather(own_block, "blk", axis=0, tiled=True), inverse_count
    )


def solution(mesh):
    placed = (P("blk", "chan"), P())
    return jax.shard_map(
        on_device,
        mesh=mesh,
        in_specs=placed,
        out_specs=P(None, "blk", None, "chan"),
        check_vma=False,
    )
```

profile of v0, /device:TPU:0, one launch (start us, length us, event | category | flops | bytes accessed | tf_op | source)
XLA Modules:
  0.0 1170.2 jit_solution(16669685366088658176)
XLA Ops:
  6.5 1.8 copy.28
  8.3 0.1 slice.80
  8.5 2.1 collective-permute-start
  10.6 33.0 %negate_multiply_fusion.3 = (f32[4096,512]{0,1:T(8,128)S(1)}, f32[4096,512]{0,1:T(8,128)S(1)}) fusion(), kind=kLoop, calls=%fused_computation.44 | loop fusion | flops 35651584 | bytes 16777216 | tf_op jit(solution)/shard_map/mul | solution.py:24
  43.7 33.8 %cosine_multiply_fusion = (f32[4096,512]{0,1:T(8,128)S(1)}, f32[4096,512]{0,1:T(8,128)S(1)}) fusion(s32[512]{0:T(512)S(1)} %iota_add_fusion), kind=kLoop, calls=%fused_computation.33 | loop fusion | flops 35651584 | bytes 16779264 | tf_op jit(solution)/shard_map/mul | solution.py:24
  77.5 37.2 %cosine_multiply_fusion.1 = (f32[4096,512]{0,1:T(8,128)}, f32[4096,512]{0,1:T(8,128)}) fusion(s32[512]{0:T(512)S(1)} %iota_add_fusion.1), kind=kLoop, calls=%fused_computation.37 | loop fusion | flops 35651584 | bytes 16779264 | tf_op jit(solution)/shard_map/mul | solution.py:24
  114.7 37.2 %cosine_multiply_fusion.2 = (f32[4096,512]{0,1:T(8,128)}, f32[4096,512]{0,1:T(8,128)}) fusion(s32[512]{0:T(512)S(1)} %iota_add_fusion.2), kind=kLoop, calls=%fused_computation.41 | loop fusion | flops 35651584 | bytes 16779264 | tf_op jit(solution)/shard_map/mul | solution.py:24
  151.9 6.2 pad_maximum_fusion.3
  158.2 13.7 %pad_maximum_fusion.2 = f32[4096,1024]{0,1:T(8,128)} fusion(f32[4096,512]{0,1:T(8,128)} %get-tuple-element.16, f32[4096,512]{0,1:T(8,128)} %get-tuple-element.15), kind=kLoop, calls=%fused_computation.4 | loop fusion | flops 4194304 | bytes 33554432 | tf_op jit(solution)/shard_map/concatenate | solution.py:24
  171.9 2.7 copy-done.1
  174.6 6.4 pad_maximum_fusion.1
  181.0 6.2 pad_maximum_fusion
  187.3 5.8 multiply_add_fusion
  193.2 22.5 %fusion.49 = bf16[8,16,2,512]{3,1,2,0:T(8,128)(2,1)} fusion(f32[2,512,4096,1]{2,1,0,3:T(8,128)} %bitcast.85, f32[8,16,4096]{2,1,0:T(8,128)S(1)} %multiply_add_fusion), kind=kOutput, calls=%fused_computation.82 | convolution fusion | flops 6442582016 | bytes 19136512 | tf_op jit(solution)/shard_map/dot_general | solution.py:53
  215.8 20.0 %fusion.46 = bf16[8,16,2,512]{3,1,2,0:T(8,128)(2,1)} fusion(f32[2,512,4096,1]{2,1,0,3:T(8,128)S(1)} %bitcast.88, f32[8,16,4096]{2,1,0:T(8,128)} %copy-done.2), kind=kOutput, calls=%fused_computation.81 | convolution fusion | flops 6442582016 | bytes 19136512 | tf_op jit(solution)/shard_map/dot_general | solution.py:53
  235.7 20.8 %fusion.43 = bf16[8,16,2,512]{3,1,2,0:T(8,128)(2,1)S(1)} fusion(f32[2,512,4096,1]{2,1,0,3:T(8,128)} %bitcast.89, f32[8,16,4096]{2,1,0:T(8,128)S(1)} %copy-done.3), kind=kOutput, calls=%fused_computation.80 | convolution fusion | flops 6442582016 | bytes 19136512 | tf_op jit(solution)/shard_map/dot_general | solution.py:53
  256.6 17.6 %fusion.40 = bf16[8,16,2,512]{3,1,2,0:T(8,128)(2,1)S(1)} fusion(f32[2,512,4096,1]{2,1,0,3:T(8,128)S(1)} %bitcast.92, f32[8,16,4096]{2,1,0:T(8,128)S(1)} %copy-done.3), kind=kOutput, calls=%fused_computation.79 | convolution fusion | flops 6442582016 | bytes 19136512 | tf_op jit(solution)/shard_map/dot_general | solution.py:53
  274.2 0.1 pad_maximum_fusion.5
  274.4 14.3 %copy.31 = bf16[8,16,2,2048]{1,2,0,3:T(2,128)(2,1)} copy(bf16[8,16,2,2048]{3,1,2,0:T(8,128)(2,1)S(1)} %pad_maximum_fusion.5) | data formatting | bytes 2097152 | tf_op jit(solution)/shard_map/concatenate | solution.py:61
  288.7 10.2 reshape.89
  298.9 17.5 %all_to_all.18 = bf16[4,2,65536]{2,1,0:T(2,128)(2,1)S(1)} all-to-all(bf16[4,2,65536]{2,1,0:T(2,128)(2,1)S(1)} %reshape.89), channel_id=1, replica_groups=mesh['chan'=4,'blk'=32] {'chan'}, dimensions={0} | all-to-all | bytes 2097152 | tf_op jit(solution)/shard_map/all_to_all | solution.py:63
  316.4 7.1 reshape.90
  323.5 19.1 %copy.42 = bf16[8,16,2,4,512]{4,3,1,2,0:T(4,128)(2,1)S(1)} copy(bf16[8,16,2,4,512]{1,2,0,4,3:T(2,128)(2,1)} %bitcast.84) | data formatting | bytes 2097152 | tf_op jit(solution)/shard_map/all_to_all | solution.py:63
  342.6 0.2 copy.33
  342.9 2.8 copy.34
  345.7 2.0 copy.41
  347.8 761.5 %all-gather.2.cloned.1.call-done = bf16[256,64,2,512]{1,0,2,3:T(8,128)(2,1)} async-done(((bf16[8,64,2,512]{1,0,2,3:T(8,128)(2,1)}), bf16[256,64,2,512]{1,0,2,3:T(8,128)(2,1)}) %all-gather.2.cloned.1.call-update) | async-done | bytes 33554448 | tf_op jit(solution)/shard_map/all_gather | solution.py:66
  1109.2 32.0 %fusion.2 = f32[8,2,256,2,512]{2,0,1,3,4:T(8,128)} fusion(bf16[8,64,2,512,1]{1,0,2,4,3:T(8,128)(2,1)S(1)} %copy.41, bf16[256,64,2,512]{1,0,2,3:T(8,128)(2,1)} %all-gather.2.cloned.1.call-done), kind=kOutput, calls=%fused_computation.18 | convolution fusion | flops 536870912 | bytes 51380224 | tf_op jit(solution)/shard_map/itpc,jtqc->ipjqc/dot_general | solution.py:28
  1141.2 4.0 fusion.29
  1145.2 4.0 fusion.31
  1149.2 3.8 maximum_multiply_fusion
  1153.0 9.9 copy.38
  (38 shorter events, 0.2 us)
Async XLA Ops:
  6.5 1102.7 %all-gather.2.cloned.1.call-start = ((), (), s32[]{:S(2)}) async-start(), calls=%async_computation.1 | async-start | bytes 69206016 | tf_op jit(solution)/shard_map/all_gather | solution.py:66
  8.5 178.8 %collective-permute-start = (bf16[8,7,4096]{2,1,0:T(8,128)(2,1)S(1)}, bf16[8,7,4096]{2,1,0:T(8,128)(2,1)}, u32[]{:S(2)}, u32[]{:S(2)}) collective-permute-start(bf16[8,7,4096]{2,1,0:T(8,128)(2,1)S(1)} %slice.80), channel_id=1, source_target_pairs={{0,32},{32,64},{64,96},{1,33},{33,65},{65,97},{2,34},{34,66},{66,9... | collective-permute-start | bytes 1376264 | tf_op jit(solution)/shard_map/ppermute | solution.py:15
  10.6 33.0 %copy-start.6 = (f32[8,4096]{1,0:T(8,128)S(1)}, f32[8,4096]{1,0:T(8,128)}, u32[]{:S(2)}) copy-start(f32[8,4096]{1,0:T(8,128)} %param.3) | copy-start | bytes 393220
  158.2 13.7 %copy-start = (f32[4096,512]{0,1:T(8,128)S(1)}, f32[4096,512]{0,1:T(8,128)}, u32[]{:S(2)}) copy-start(f32[4096,512]{0,1:T(8,128)} %get-tuple-element.13) | copy-start | bytes 25165828
  158.2 16.5 %copy-start.1 = (f32[4096,512]{0,1:T(8,128)S(1)}, f32[4096,512]{0,1:T(8,128)}, u32[]{:S(2)}) copy-start(f32[4096,512]{0,1:T(8,128)} %get-tuple-element.14) | copy-start | bytes 25165828
  187.3 28.4 %slice-start = ((s8[16777216]{0:T(1024)(128)(4,1)}), s8[4194304]{0:T(1024)(128)(4,1)S(1)}, s32[]{:S(2)}) async-start(s8[16777216]{0:T(1024)(128)(4,1)} %bitcast.86), calls=%async_computation.2 | async-start | bytes 8388608
  193.1 22.5 %copy-start.2 = (f32[8,16,4096]{2,1,0:T(8,128)}, f32[8,16,4096]{2,1,0:T(8,128)S(1)}, u32[]{:S(2)}) copy-start(f32[8,16,4096]{2,1,0:T(8,128)S(1)} %multiply_add_fusion) | copy-start | bytes 6291460
  193.1 22.5 %slice-start.1 = ((s8[16777216]{0:T(1024)(128)(4,1)}), s8[4194304]{0:T(1024)(128)(4,1)S(1)}, s32[]{:S(2)}) async-start(s8[16777216]{0:T(1024)(128)(4,1)} %bitcast.86), calls=%async_computation.3 | async-start | bytes 8388608
  193.2 22.5 %slice-start.2 = ((s8[16777216]{0:T(1024)(128)(4,1)}), s8[4194304]{0:T(1024)(128)(4,1)S(1)}, s32[]{:S(2)}) async-start(s8[16777216]{0:T(1024)(128)(4,1)} %bitcast.86), calls=%async_computation.4 | async-start | bytes 8388608
  193.2 22.5 %slice-start.3 = ((s8[16777216]{0:T(1024)(128)(4,1)}), s8[4194304]{0:T(1024)(128)(4,1)S(1)}, s32[]{:S(2)}) async-start(s8[16777216]{0:T(1024)(128)(4,1)} %bitcast.86), calls=%async_computation.5 | async-start | bytes 8388608
  215.7 20.0 %copy-start.3 = (f32[8,16,4096]{2,1,0:T(8,128)S(1)}, f32[8,16,4096]{2,1,0:T(8,128)}, u32[]{:S(2)}) copy-start(f32[8,16,4096]{2,1,0:T(8,128)} %copy-done.2) | copy-start | bytes 6291460
  215.7 40.8 %slice-start.4 = ((s8[16777216]{0:T(1024)(128)(4,1)}), s8[4194304]{0:T(1024)(128)(4,1)S(1)}, s32[]{:S(2)}) async-start(s8[16777216]{0:T(1024)(128)(4,1)} %bitcast.90), calls=%async_computation.6 | async-start | bytes 8388608
  215.7 40.8 %slice-start.5 = ((s8[16777216]{0:T(1024)(128)(4,1)}), s8[4194304]{0:T(1024)(128)(4,1)S(1)}, s32[]{:S(2)}) async-start(s8[16777216]{0:T(1024)(128)(4,1)} %bitcast.90), calls=%async_computation.7 | async-start | bytes 8388608
  235.7 20.8 %slice-start.6 = ((s8[16777216]{0:T(1024)(128)(4,1)}), s8[4194304]{0:T(1024)(128)(4,1)S(1)}, s32[]{:S(2)}) async-start(s8[16777216]{0:T(1024)(128)(4,1)} %bitcast.90), calls=%async_computation.8 | async-start | bytes 8388608
  235.7 20.8 %slice-start.7 = ((s8[16777216]{0:T(1024)(128)(4,1)}), s8[4194304]{0:T(1024)(128)(4,1)S(1)}, s32[]{:S(2)}) async-start(s8[16777216]{0:T(1024)(128)(4,1)} %bitcast.90), calls=%async_computation.9 | async-start | bytes 8388608
  256.6 17.6 %copy-start.4 = (bf16[8,16,2,512]{3,1,2,0:T(8,128)(2,1)S(1)}, bf16[8,16,2,512]{3,1,2,0:T(8,128)(2,1)}, u32[]{:S(2)}) copy-start(bf16[8,16,2,512]{3,1,2,0:T(8,128)(2,1)} %fusion.49) | copy-start | bytes 786436
  256.6 17.6 %copy-start.5 = (bf16[8,16,2,512]{3,1,2,0:T(8,128)(2,1)S(1)}, bf16[8,16,2,512]{3,1,2,0:T(8,128)(2,1)}, u32[]{:S(2)}) copy-start(bf16[8,16,2,512]{3,1,2,0:T(8,128)(2,1)} %fusion.46) | copy-start | bytes 786436
Sparse Core Ops, SparseCore 0:
  345.8 763.3 all-gather.1
where the time goes:
time: 1180 us; the launch traced here: 1170 us
  waiting for transfers between devices  761 us (64%)
  other arithmetic  192 us (16%)
  matrix products  113 us (10%)
  local copies, waits for them, and re-layouts  70.6 us (6%)
  blocking collectives  17.5 us (1%)
  between operations  14.1 us (1%)
    all_gather x1, waiting for transfers between devices, on_device(): lax.all_gather(own_block, 'blk', axis=0, tiled=True)  761 us
    mul x3, other arithmetic, dft_table(): jnp.cos(angles) * normaliser  108 us
    dot_general x4, matrix products, on_device(): jnp.dot(frame_rows, cos_sin_table, precision=lax.Precision.HIGHEST, prefe...  80.8 us
    mul x1, other arithmetic, dft_table(): -jnp.sin(angles) * normaliser  33 us
    concatenate x4, other arithmetic, dft_table(): jnp.concatenate([jnp.cos(angles) * normaliser, -jnp.sin(angles) * normali...  32.6 us
    dot_general x1, matrix products, correlate_pair(): jnp.einsum('itpc,jtqc->ipjqc', left_block, right_block, preferred_element...  32 us
    all_to_all x4, local copies, waits for them, and re-layouts, on_device(): lax.all_to_all(spectra, 'chan', split_axis=3, concat_axis=1, tiled=True)  24.2 us
  transfers between devices with their start and end apart: 2, of which 1 were waited for; matrix products, arithmetic and copies ran while one was open for 15% of the time, Pallas kernels for 0%

commit v1 on v0

--- a/solution.py
+++ b/solution.py
@@ -63,7 +63,11 @@
     own_block = lax.all_to_all(spectra, "chan", split_axis=3, concat_axis=1, tiled=True)
     inverse_count = 1.0 / own_block.shape[1]
     return correlate_pair(
-        own_block, lax.all_gather(own_block, "blk", axis=0, tiled=True), inverse_count
+        own_block,
+        jnp.concatenate(
+            lax.all_to_all(jnp.stack([own_block] * lax.axis_size("blk")), "blk", 0, 0), axis=0
+        ),
+        inverse_count,
     )
 
 

time: 1180 us -> 1100 us (0.932)
  the two profiles are of different devices: /device:TPU:0 before, /device:TPU:40 now
where the time goes in v1:
time: 1100 us; the launch traced here: 1090 us
  waiting for transfers between devices  630 us (57%)
  other arithmetic  206 us (19%)
  local copies, waits for them, and re-layouts  127 us (12%)
  matrix products  99.7 us (9%)
  blocking collectives  15.8 us (1%)
  starting transfers between devices  12.2 us (1%)
    all_to_all x1, waiting for transfers between devices, on_device(): lax.all_to_all(jnp.stack([own_block] * lax.axis_size('blk')), 'blk', 0, 0)  630 us
    mul x3, other arithmetic, dft_table(): jnp.cos(angles) * normaliser  119 us
    dot_general x4, matrix products, on_device(): jnp.dot(frame_rows, cos_sin_table, precision=lax.Precision.HIGHEST, prefe...  80.8 us
    reshape x1, local copies, waits for them, and re-layouts, on_device(): jnp.concatenate(lax.all_to_all(jnp.stack([own_block] * lax.axis_size('blk...  50.8 us
    concatenate x4, other arithmetic, dft_table(): jnp.concatenate([jnp.cos(angles) * normaliser, -jnp.sin(angles) * normali...  36.6 us
    mul x1, other arithmetic, dft_table(): -jnp.sin(angles) * normaliser  33 us
  transfers between devices with their start and end apart: 2, of which 1 were waited for; matrix products, arithmetic and copies ran while one was open for 17% of the time, Pallas kernels for 0%

profile of v1, /device:TPU:40, one launch (start us, length us, event | category | flops | bytes accessed | tf_op | source)
XLA Modules:
  0.0 1091.1 jit_solution(1122099602776420384)
XLA Ops:
  0.0 1.8 copy.29
  1.9 1.9 collective-permute-start
  3.9 33.0 %negate_multiply_fusion.3 = (f32[4096,512]{0,1:T(8,128)S(1)}, f32[4096,512]{0,1:T(8,128)S(1)}) fusion(), kind=kLoop, calls=%fused_computation.42 | loop fusion | flops 35651584 | bytes 16777216 | tf_op jit(solution)/shard_map/mul | solution.py:24
  37.0 37.2 %cosine_multiply_fusion.2 = (f32[4096,512]{0,1:T(8,128)}, f32[4096,512]{0,1:T(8,128)}) fusion(s32[512]{0:T(512)S(1)} %iota_add_fusion.2), kind=kLoop, calls=%fused_computation.39 | loop fusion | flops 35651584 | bytes 16779264 | tf_op jit(solution)/shard_map/mul | solution.py:24
  74.3 37.2 %cosine_multiply_fusion.1 = (f32[4096,512]{0,1:T(8,128)}, f32[4096,512]{0,1:T(8,128)}) fusion(s32[512]{0:T(512)S(1)} %iota_add_fusion.1), kind=kLoop, calls=%fused_computation.35 | loop fusion | flops 35651584 | bytes 16779264 | tf_op jit(solution)/shard_map/mul | solution.py:24
  111.5 44.3 %cosine_multiply_fusion = (f32[4096,512]{0,1:T(8,128)S(1)}, f32[4096,512]{0,1:T(8,128)S(1)}) fusion(s32[512]{0:T(512)S(1)} %iota_add_fusion), kind=kLoop, calls=%fused_computation.31 | loop fusion | flops 35651584 | bytes 16779264 | tf_op jit(solution)/shard_map/mul | solution.py:24
  155.8 11.9 %pad_maximum_fusion.1 = f32[4096,1024]{0,1:T(8,128)} fusion(f32[4096,512]{0,1:T(8,128)} %get-tuple-element.14, f32[4096,512]{0,1:T(8,128)} %get-tuple-element.13), kind=kLoop, calls=%fused_computation.1 | loop fusion | flops 4194304 | bytes 33554432 | tf_op jit(solution)/shard_map/concatenate | solution.py:24
  167.7 11.9 %pad_maximum_fusion.2 = f32[4096,1024]{0,1:T(8,128)} fusion(f32[4096,512]{0,1:T(8,128)} %get-tuple-element.16, f32[4096,512]{0,1:T(8,128)} %get-tuple-element.15), kind=kLoop, calls=%fused_computation.2 | loop fusion | flops 4194304 | bytes 33554432 | tf_op jit(solution)/shard_map/concatenate | solution.py:24
  179.6 6.4 pad_maximum_fusion
  185.9 6.4 pad_maximum_fusion.3
  192.3 5.6 multiply_add_fusion
  198.0 22.5 %fusion.38 = bf16[8,16,2,512]{3,1,2,0:T(8,128)(2,1)} fusion(f32[2,512,4096,1]{2,1,0,3:T(8,128)} %bitcast.82, f32[8,16,4096]{2,1,0:T(8,128)S(1)} %multiply_add_fusion), kind=kOutput, calls=%fused_computation.78 | convolution fusion | flops 6442582016 | bytes 19136512 | tf_op jit(solution)/shard_map/dot_general | solution.py:53
  220.6 20.0 %fusion.41 = bf16[8,16,2,512]{3,1,2,0:T(8,128)(2,1)} fusion(f32[2,512,4096,1]{2,1,0,3:T(8,128)S(1)} %bitcast.85, f32[8,16,4096]{2,1,0:T(8,128)} %copy-done), kind=kOutput, calls=%fused_computation.79 | convolution fusion | flops 6442582016 | bytes 19136512 | tf_op jit(solution)/shard_map/dot_general | solution.py:53
  240.6 20.8 %fusion.35 = bf16[8,16,2,512]{3,1,2,0:T(8,128)(2,1)S(1)} fusion(f32[2,512,4096,1]{2,1,0,3:T(8,128)} %bitcast.86, f32[8,16,4096]{2,1,0:T(8,128)S(1)} %copy-done.1), kind=kOutput, calls=%fused_computation.77 | convolution fusion | flops 6442582016 | bytes 19136512 | tf_op jit(solution)/shard_map/dot_general | solution.py:53
  261.5 17.6 %fusion.44 = bf16[8,16,2,512]{3,1,2,0:T(8,128)(2,1)S(1)} fusion(f32[2,512,4096,1]{2,1,0,3:T(8,128)S(1)} %bitcast.89, f32[8,16,4096]{2,1,0:T(8,128)S(1)} %copy-done.1), kind=kOutput, calls=%fused_computation.80 | convolution fusion | flops 6442582016 | bytes 19136512 | tf_op jit(solution)/shard_map/dot_general | solution.py:53
  279.1 0.1 pad_maximum_fusion.5
  279.2 14.3 %copy.32 = bf16[8,16,2,2048]{1,2,0,3:T(2,128)(2,1)} copy(bf16[8,16,2,2048]{3,1,2,0:T(8,128)(2,1)S(1)} %pad_maximum_fusion.5) | data formatting | bytes 2097152 | tf_op jit(solution)/shard_map/concatenate | solution.py:61
  293.5 10.2 reshape.96
  303.8 15.8 %all_to_all.20 = bf16[4,2,65536]{2,1,0:T(2,128)(2,1)S(1)} all-to-all(bf16[4,2,65536]{2,1,0:T(2,128)(2,1)S(1)} %reshape.96), channel_id=1, replica_groups=mesh['chan'=4,'blk'=32] {'chan'}, dimensions={0} | all-to-all | bytes 2097152 | tf_op jit(solution)/shard_map/all_to_all | solution.py:63
  319.6 7.1 reshape.97
  326.7 19.1 %copy.43 = bf16[8,16,2,4,512]{4,3,1,2,0:T(4,128)(2,1)S(1)} copy(bf16[8,16,2,4,512]{1,2,0,4,3:T(2,128)(2,1)} %bitcast.81) | data formatting | bytes 2097152 | tf_op jit(solution)/shard_map/all_to_all | solution.py:63
  345.8 0.2 copy.34
  346.1 11.1 %stack.7 = bf16[32,8,64,2,512]{4,2,3,1,0:T(8,128)(2,1)} broadcast(bf16[8,64,2,512]{3,1,2,0:T(8,128)(2,1)S(1)} %bitcast.90), dimensions={1,2,3,4} | broadcast | bytes 34603008 | tf_op jit(solution)/shard_map/stack | solution.py:68
  357.2 10.3 all-to-all-start.1
  367.5 2.0 copy.42
  369.5 629.9 %all-to-all-done.1 = bf16[32,8,64,2,512]{4,2,3,1,0:T(8,128)(2,1)} async-done(((bf16[32,8,64,2,512]{4,2,3,1,0:T(8,128)(2,1)}), bf16[32,8,64,2,512]{4,2,3,1,0:T(8,128)(2,1)}, u32[]{:S(2)}, u32[]{:S(2)}) %all-to-all-start.1) | async-done | bytes 33554464 | tf_op jit(solution)/shard_map/all_to_all | solution.py:68
  999.4 50.8 %copy.41 = bf16[256,64,2,512,1]{0,1,4,2,3:T(8,128)(2,1)} copy(bf16[256,64,2,512,1]{3,1,2,0,4:T(8,128)(2,1)} %bitcast.28) | data formatting | bytes 67108864 | tf_op jit(solution)/shard_map/reshape | solution.py:67
  1050.1 18.9 %convolution_bitcast_fusion = f32[8,2,256,2,512]{2,0,1,3,4:T(8,128)} fusion(bf16[256,64,2,512,1]{0,1,4,2,3:T(8,128)(2,1)} %copy.41, bf16[8,64,2,512,1]{1,0,2,4,3:T(8,128)(2,1)S(1)} %copy.42), kind=kOutput, calls=%fused_computation.16 | convolution fusion | flops 536870912 | bytes 51380224 | tf_op jit(solution)/shard_map/itpc,jtqc->ipjqc/dot_general | solution.py:28
  1069.0 4.0 fusion.24
  1073.0 4.0 fusion.26
  1077.0 3.8 maximum_multiply_fusion
  1080.9 9.9 copy.39
  (34 shorter events, 0.3 us)
Async XLA Ops:
  1.9 190.4 %collective-permute-start = (bf16[8,7,4096]{2,1,0:T(8,128)(2,1)S(1)}, bf16[8,7,4096]{2,1,0:T(8,128)(2,1)}, u32[]{:S(2)}, u32[]{:S(2)}) collective-permute-start(bf16[8,7,4096]{2,1,0:T(8,128)(2,1)S(1)} %slice.80), channel_id=1, source_target_pairs={{0,32},{32,64},{64,96},{1,33},{33,65},{65,97},{2,34},{34,66},{66,9... | collective-permute-start | bytes 1376264 | tf_op jit(solution)/shard_map/ppermute | solution.py:15
  3.9 33.0 %copy-start.4 = (f32[8,4096]{1,0:T(8,128)S(1)}, f32[8,4096]{1,0:T(8,128)}, u32[]{:S(2)}) copy-start(f32[8,4096]{1,0:T(8,128)} %param.3) | copy-start | bytes 393220
  192.3 28.2 %slice-start = ((s8[16777216]{0:T(1024)(128)(4,1)}), s8[4194304]{0:T(1024)(128)(4,1)S(1)}, s32[]{:S(2)}) async-start(s8[16777216]{0:T(1024)(128)(4,1)} %bitcast.83), calls=%async_computation.2 | async-start | bytes 8388608
  198.0 22.5 %copy-start = (f32[8,16,4096]{2,1,0:T(8,128)}, f32[8,16,4096]{2,1,0:T(8,128)S(1)}, u32[]{:S(2)}) copy-start(f32[8,16,4096]{2,1,0:T(8,128)S(1)} %multiply_add_fusion) | copy-start | bytes 6291460
  198.0 22.5 %slice-start.1 = ((s8[16777216]{0:T(1024)(128)(4,1)}), s8[4194304]{0:T(1024)(128)(4,1)S(1)}, s32[]{:S(2)}) async-start(s8[16777216]{0:T(1024)(128)(4,1)} %bitcast.83), calls=%async_computation.3 | async-start | bytes 8388608
  198.0 22.5 %slice-start.2 = ((s8[16777216]{0:T(1024)(128)(4,1)}), s8[4194304]{0:T(1024)(128)(4,1)S(1)}, s32[]{:S(2)}) async-start(s8[16777216]{0:T(1024)(128)(4,1)} %bitcast.83), calls=%async_computation.4 | async-start | bytes 8388608
  198.0 22.5 %slice-start.3 = ((s8[16777216]{0:T(1024)(128)(4,1)}), s8[4194304]{0:T(1024)(128)(4,1)S(1)}, s32[]{:S(2)}) async-start(s8[16777216]{0:T(1024)(128)(4,1)} %bitcast.83), calls=%async_computation.5 | async-start | bytes 8388608
  220.6 20.0 %copy-start.1 = (f32[8,16,4096]{2,1,0:T(8,128)S(1)}, f32[8,16,4096]{2,1,0:T(8,128)}, u32[]{:S(2)}) copy-start(f32[8,16,4096]{2,1,0:T(8,128)} %copy-done) | copy-start | bytes 6291460
  220.6 40.8 %slice-start.4 = ((s8[16777216]{0:T(1024)(128)(4,1)}), s8[4194304]{0:T(1024)(128)(4,1)S(1)}, s32[]{:S(2)}) async-start(s8[16777216]{0:T(1024)(128)(4,1)} %bitcast.87), calls=%async_computation.6 | async-start | bytes 8388608
  220.6 40.8 %slice-start.5 = ((s8[16777216]{0:T(1024)(128)(4,1)}), s8[4194304]{0:T(1024)(128)(4,1)S(1)}, s32[]{:S(2)}) async-start(s8[16777216]{0:T(1024)(128)(4,1)} %bitcast.87), calls=%async_computation.7 | async-start | bytes 8388608
  240.6 20.8 %slice-start.6 = ((s8[16777216]{0:T(1024)(128)(4,1)}), s8[4194304]{0:T(1024)(128)(4,1)S(1)}, s32[]{:S(2)}) async-start(s8[16777216]{0:T(1024)(128)(4,1)} %bitcast.87), calls=%async_computation.8 | async-start | bytes 8388608
  240.6 20.8 %slice-start.7 = ((s8[16777216]{0:T(1024)(128)(4,1)}), s8[4194304]{0:T(1024)(128)(4,1)S(1)}, s32[]{:S(2)}) async-start(s8[16777216]{0:T(1024)(128)(4,1)} %bitcast.87), calls=%async_computation.9 | async-start | bytes 8388608
  261.4 17.6 %copy-start.2 = (bf16[8,16,2,512]{3,1,2,0:T(8,128)(2,1)S(1)}, bf16[8,16,2,512]{3,1,2,0:T(8,128)(2,1)}, u32[]{:S(2)}) copy-start(bf16[8,16,2,512]{3,1,2,0:T(8,128)(2,1)} %fusion.38) | copy-start | bytes 786436
  261.4 17.6 %copy-start.3 = (bf16[8,16,2,512]{3,1,2,0:T(8,128)(2,1)S(1)}, bf16[8,16,2,512]{3,1,2,0:T(8,128)(2,1)}, u32[]{:S(2)}) copy-start(bf16[8,16,2,512]{3,1,2,0:T(8,128)(2,1)} %fusion.41) | copy-start | bytes 786436
  357.2 642.2 %all-to-all-start.1 = ((bf16[32,8,64,2,512]{4,2,3,1,0:T(8,128)(2,1)}), bf16[32,8,64,2,512]{4,2,3,1,0:T(8,128)(2,1)}, u32[]{:S(2)}, u32[]{:S(2)}) async-start(bf16[32,8,64,2,512]{4,2,3,1,0:T(8,128)(2,1)} %stack.7), calls=%async_computation.1 | async-start | bytes 67108864 | tf_op jit(solution)/shard_map/all_to_all | solution.py:68
